TPU v7x, 256 devices: a whole 4x4x8 slice. The times are simulated.
256 devices in a mesh: row: 4 (over y), col: 4 (over x), dp: 16 (over z, core).
Axes of the slice: x: 4, y: 4, z: 8, core: 2. Of those that a mesh axis runs over, the one named last changes fastest.
Arguments:
- hidden_states: bfloat16 [16384, 1536], P(('dp', 'row'), 'col'), may hold values from -18 to 18
- w_query: bfloat16 [1536, 1536], P('col', 'row'), may hold values from -0.102062073 to 0.102062073
- w_key_value: bfloat16 [1536, 512], P('col'), may hold values from -0.102062073 to 0.102062073
- adapter_down: bfloat16 [1024, 1536, 16], P('dp', 'col'), may hold values from -0.15625 to 0.15625
- adapter_up: bfloat16 [1024, 16, 1536], P('dp', None, 'row'), may hold values from -1.5 to 1.5
- req_lengths: int32 [16, 8], replicated, may hold values from 1 to 160, 960 in all within a row
- req_adapter: int32 [16, 8], replicated, may hold values from 0 to 1023, as said below
Outputs:
- attention: bfloat16 [16384, 1536], P(('dp', 'col'), 'row')
- kv_cache: bfloat16 [16384, 512], P(('dp', 'col'))
Inputs may be any that keep to these rules, and one draw needn't show every extreme that they name: `req_lengths`: the lengths of one block sum to 960, and each block has a request of exactly 160 tokens. `req_adapter`: adapters k * 64 to (k + 1) * 64 - 1 are those of index k of dp; the requests of one block use adapters of one index of dp at most 1 times, and some index of dp is used exactly that often by every block.
All inputs are finite; a program needn't handle non-finite values.
Results may differ from a plain program's by a relative error of at most 0.0072.
Values may be sent and summed in bfloat16 or wider, within the bound.
No kernel may reach another device: no remote copies, remote signals or barrier semaphores. Data moves between devices by JAX's collectives and lax.ppermute only.
A program may use at most 128 MiB of HBM per device.

v0:
```python
import math
import jax
import jax.numpy as jnp
from jax import lax
from jax.sharding import PartitionSpec as P

HEAD_DIM = 128
MOST_LEN = 160
masked_score = -1e30


def block_layout(lengths_row, block_len):
    prefix_len = block_len - jnp.sum(lengths_row)
    ends_at = jnp.cumsum(lengths_row) + prefix_len
    starts = ends_at - lengths_row
    positions = jnp.arange(block_len, dtype=jnp.int32)
    segment = jnp.sum((positions[:, None] >= starts[None, :]).astype(jnp.int32), axis=1)
    return (starts, segment, positions)


def slot_numbers(holders):
    request_total = holders.shape[0]
    ordering = jnp.arange(request_total, dtype=jnp.int32)
    earlier = ordering[None, :] < ordering[:, None]
    same_holder = holders[:, None] == holders[None, :]
    return jnp.sum((earlier & same_holder).astype(jnp.int32), axis=1)


def make_attend(query_rows, segment, first_row, kv_group, head_size, kv_half):
    own_rows = query_rows.shape[0]
    heads_here = query_rows.shape[1] // head_size
    query_heads = query_rows.reshape(own_rows, heads_here, head_size)
    query_pos = first_row + jnp.arange(own_rows, dtype=jnp.int32)
    query_seg = lax.dynamic_slice_in_dim(segment, first_row, own_rows, 0)
    score_scale = 1.0 / math.sqrt(head_size)

    def attend(state_in, key_block, key_start):
        running_max, running_sum, running_out = state_in
        block_size = key_block.shape[0]
        key_rows = lax.dynamic_slice_in_dim(key_block, kv_group * head_size, head_size, 1)
        values = lax.dynamic_slice_in_dim(key_block, kv_half + kv_group * head_size, head_size, 1)
        key_pos = jnp.arange(block_size, dtype=jnp.int32)
        allowed = (key_pos[None, :] <= query_pos[:, None]) & (
            (segment[None, :] == query_seg[:, None]) | (segment[None, :] == 0)
        )
        scores = (
            jnp.einsum("qhd,kd->hqk", query_heads, key_rows, preferred_element_type=jnp.float32)
            * score_scale
        )
        scores = jnp.where(allowed[None], scores, masked_score)
        new_max = jnp.maximum(running_max, jnp.max(scores, axis=2))
        weights = jnp.where(allowed[None], jnp.exp(scores - new_max[:, :, None]), 0.0)
        running_sum = jnp.sum(weights, axis=2)
        running_out = jnp.einsum(
            "hqk,kd->hqd", weights.astype(jnp.bfloat16), values, preferred_element_type=jnp.float32
        )
        return (new_max, running_sum, running_out)

    initial = (
        jnp.full((heads_here, own_rows), masked_score, jnp.float32),
        jnp.zeros((heads_here, own_rows), jnp.float32),
        jnp.zeros((heads_here, own_rows, head_size), jnp.float32),
    )
    return (attend, initial)


def body(hidden_states, w_query, w_key_value, adapter_down, adapter_up, req_lengths, req_adapter):
    dp_size = lax.axis_size("dp")
    block_index = lax.axis_index("dp")
    col_index = lax.axis_index("col")
    row_index = lax.axis_index("row")
    gathered = lax.all_gather(hidden_states, "row", axis=0, tiled=True)
    block_len = gathered.shape[0]
    query_cols = w_query.shape[1]
    kv_cols = w_key_value.shape[1]
    kv_half = kv_cols // 2
    head_size = HEAD_DIM
    heads_here = query_cols // head_size
    heads_total = heads_here * lax.axis_size("row")
    kv_heads = kv_half // head_size
    kv_group = row_index * heads_here // (heads_total // kv_heads)
    own_rows = block_len // lax.axis_size("col")
    first_row = col_index * own_rows
    held_sets = adapter_down.shape[0]
    width_here = adapter_down.shape[1]
    rank_size = adapter_down.shape[2]
    lengths_row = req_lengths[block_index]
    adapters_row = req_adapter[block_index]
    requests = lengths_row.shape[0]
    starts, segment, positions = block_layout(lengths_row, block_len)
    request_of = jnp.clip(segment - 1, 0, requests - 1)
    in_request = segment > 0
    holders = adapters_row // held_sets
    wanted_from_me = req_adapter // held_sets == block_index
    local_pick = jnp.sum(jnp.where(wanted_from_me, req_adapter % held_sets, 0), axis=1)
    down_pick = jnp.transpose(jnp.take(adapter_down, local_pick, axis=0), (0, 2, 1))
    up_pick = jnp.take(adapter_up, local_pick, axis=0)
    outgoing = jnp.concatenate([down_pick, up_pick], axis=1)
    incoming = lax.all_to_all(outgoing, "dp", split_axis=0, concat_axis=0, tiled=True)
    flat_down = incoming[:, :rank_size, :].reshape(dp_size * rank_size, width_here).T
    flat_up = (
        incoming[:, rank_size:, :].reshape(dp_size * rank_size, query_cols).astype(jnp.float32)
    )
    rank_owner = jnp.arange(dp_size * rank_size, dtype=jnp.int32) // rank_size
    reduced = jnp.dot(gathered, flat_down, preferred_element_type=jnp.float32)
    request_ids = jnp.arange(requests, dtype=jnp.int32)
    token_holder = (
        jnp.sum(
            jnp.where(segment[:, None] == request_ids[None, :] + 1, holders[None, :] + 1, 0), axis=1
        )
        - 1
    )
    kept_cols = rank_owner[None, :] == token_holder[:, None]
    reduced = jnp.where(kept_cols, reduced, 0.0)
    adapter_term = jnp.dot(reduced, flat_up, precision=lax.Precision.HIGHEST)
    kv_share = kv_cols // lax.axis_size("row")
    kv_slice = lax.dynamic_slice_in_dim(w_key_value, row_index * kv_share, kv_share, 1)
    both_weights = jnp.concatenate([w_query, kv_slice], axis=1)
    partial_value = jnp.dot(gathered, both_weights, preferred_element_type=jnp.float32)
    summed = lax.psum_scatter(
        partial_value
        + jnp.concatenate(
            [adapter_term, jnp.zeros((own_rows * lax.axis_size("col"), kv_share), jnp.float32)],
            axis=1,
        ),
        "col",
        scatter_dimension=0,
        tiled=True,
    )
    query_rows = summed[:, :query_cols].astype(jnp.bfloat16)
    kv_pieces = lax.all_gather(summed[:, query_cols:].astype(jnp.bfloat16), ("row", "col"), axis=0)
    kv_pieces = kv_pieces.reshape(lax.axis_size("row"), lax.axis_size("col"), own_rows, kv_share)
    own_pieces = lax.dynamic_index_in_dim(kv_pieces, col_index, 1, keepdims=False)
    kv_cache = jnp.transpose(own_pieces, (1, 0, 2)).reshape(own_rows, kv_cols)
    parts_per_head = head_size // kv_share
    key_all = lax.dynamic_slice_in_dim(kv_pieces, kv_group * parts_per_head, parts_per_head, 0)
    value_all = lax.dynamic_slice_in_dim(
        kv_pieces, (kv_heads + kv_group) * parts_per_head, parts_per_head, 0
    )
    key_all = jnp.transpose(key_all, (1, 2, 0, 3)).reshape(block_len, head_size)
    value_all = jnp.transpose(value_all, (1, 2, 0, 3)).reshape(block_len, head_size)
    attend, initial = make_attend(query_rows, segment, first_row, 0, head_size, head_size)
    running_max, running_sum, running_out = attend(
        initial, jnp.concatenate([key_all, value_all], axis=1), jnp.int32(0)
    )
    attention = (running_out / running_sum[:, :, None]).astype(jnp.bfloat16)
    attention = jnp.transpose(attention, (1, 0, 2)).reshape(own_rows, query_cols)
    return (attention, kv_cache)


def solution(mesh):
    return jax.shard_map(
        body,
        mesh=mesh,
        in_specs=(
            P(("dp", "row"), "col"),
            P("col", "row"),
            P("col", None),
            P("dp", "col", None),
            P("dp", None, "row"),
            P(),
            P(),
        ),
        out_specs=(P(("dp", "col"), "row"), P(("dp", "col"), None)),
        check_vma=False,
    )
```

profile of v0, /device:TPU:2, one launch (start us, length us, event | category | flops | bytes accessed | tf_op | source)
XLA Modules:
  0.0 139.3 jit_solution(9572171960682573029)
XLA Ops:
  7.2 0.0 copy-start
  7.2 0.0 copy-start.3
  7.2 0.0 copy-start.4
  7.2 0.0 copy-start.2
  7.2 0.8 fusion.25
  8.0 0.3 copy-done
  8.3 0.6 gather_fusion.1
  8.9 1.7 %gather_fusion = bf16[16,384,16]{1,2,0:T(8,128)(2,1)S(1)} fusion(bf16[64,384,16]{1,2,0:T(8,128)(2,1)} %param.10, s32[1024]{0:T(1024)S(1)} %pad_clamp_fusion), kind=kCustom, calls=%fused_computation | custom fusion | bytes 393280 | tf_op jit(solution)/shard_map/jit(_take)/gather | solution.py:96
  10.6 0.1 broadcast_select_fusion
  10.7 0.1 select_bitcast_fusion
  10.9 0.8 pad_maximum_fusion
  11.6 8.6 %all-to-all-start = ((bf16[16,32,384]{2,1,0:T(8,128)(2,1)}), bf16[16,32,384]{2,1,0:T(8,128)(2,1)S(1)}, u32[]{:S(2)}, u32[]{:S(2)}) async-start(bf16[16,32,384]{2,1,0:T(8,128)(2,1)} %pad_maximum_fusion), calls=%async_computation | async-start | bytes 786432 | tf_op jit(solution)/shard_map/all_to_all | solution.py:99
  20.2 0.0 reduce-scatter.2.cloned.1.call-start
  20.3 0.0 copy-done.3
  20.3 0.0 copy-done.4
  20.3 0.7 fusion.34
  21.7 0.1 subtract_reduce_fusion
  21.8 0.1 convert_reduce_fusion
  21.9 0.9 constant_dynamic-slice_fusion.3
  22.8 0.1 select_reduce_fusion
  22.9 0.0 copy-done.2
  22.9 0.0 copy-start.1
  22.9 14.5 %all_gather.9 = bf16[1024,384]{1,0:T(8,128)(2,1)S(1)} all-gather(bf16[256,384]{1,0:T(8,128)(2,1)S(1)} %copy-done.2), channel_id=1, replica_groups=mesh['row'=4,'col'=4,'dp'=16] {'row'}, dimensions={0}, use_global_device_ids=true | all-gather | bytes 983040 | tf_op jit(solution)/shard_map/all_gather | solution.py:72
  37.4 0.0 all-to-all-done
  37.4 0.5 fusion.6
  37.9 0.9 fusion.36
  38.8 0.0 copy-done.1
  38.8 2.1 %bitcast_add_fusion = f32[1024,512]{0,1:T(8,128)} fusion(f32[1024,384]{0,1:T(8,128)S(1)} %fusion.36, bf16[1024,384]{1,0:T(8,128)(2,1)S(1)} %all_gather.9, bf16[384,128]{1,0:T(8,128)(2,1)S(1)} %constant_dynamic-slice_fusion.3, bf16[384,384]{1,0:T(8,128)(2,1)S(1)} %copy-done.1), kind=kOutput, calls=%fused_computation.7 | convolution fusion | flops 403963904 | bytes 4849664 | tf_op jit(solution)/shard_map/dot_general | solution.py:119
  40.9 0.0 reduce-scatter.2.cloned.1.call-update
  41.0 0.0 all-gather.3.cloned.1.call-start
  41.0 32.3 %reduce-scatter.2.cloned.1.call-done = f32[256,512]{0,1:T(8,128)} async-done(((f32[1024,512]{0,1:T(8,128)}), f32[256,512]{0,1:T(8,128)}) %reduce-scatter.2.cloned.1.call-update) | async-done | bytes 524304 | tf_op jit(solution)/shard_map/reduce_scatter | solution.py:120
  73.3 1.1 convert.4
  74.4 0.6 slice.24
  75.0 0.0 all-gather.3.cloned.1.call-update
  75.1 0.1 dynamic_slice.23
  75.2 0.8 fusion.10
  76.0 49.1 %all-gather.3.cloned.1.call-done = bf16[4096,128]{0,1:T(8,128)(2,1)} async-done(((bf16[256,128]{0,1:T(8,128)(2,1)}), bf16[4096,128]{0,1:T(8,128)(2,1)}) %all-gather.3.cloned.1.call-update) | async-done | bytes 1048592 | tf_op jit(solution)/shard_map/all_gather | solution.py:131
  125.1 1.8 %reshape.151 = bf16[4,4,256,128]{2,1,0,3:T(4,128)(2,1)S(1)} reshape(bf16[4096,128]{0,1:T(8,128)(2,1)} %all-gather.3.cloned.1.call-done) | data formatting | bytes 2097152 | tf_op jit(solution)/shard_map/reshape | solution.py:132
  127.0 0.5 constant_dynamic-slice_fusion.2
  127.6 0.1 copy.40
  127.6 0.8 copy.35
  128.5 0.2 constant_dynamic-slice_fusion.1
  128.7 0.2 copy.29
  128.9 0.2 reshape.174
  129.1 0.7 fusion
  129.8 0.8 fusion.1
  130.6 1.0 fusion.14
  131.6 0.8 copy.34
  (12 shorter events, 0.1 us)
Async XLA Ops:
  7.2 1.2 copy-start
  7.2 13.1 %copy-start.3 = (s32[16,8]{0,1:T(8,128)S(1)}, s32[16,8]{0,1:T(8,128)}, u32[]{:S(2)}) copy-start(s32[16,8]{0,1:T(8,128)} %param.13) | copy-start | bytes 1540
  7.2 13.1 %copy-start.4 = (s32[16,8]{0,1:T(8,128)S(1)}, s32[16,8]{0,1:T(8,128)}, u32[]{:S(2)}) copy-start(s32[16,8]{0,1:T(8,128)} %param.12) | copy-start | bytes 1540
  7.2 15.7 %copy-start.2 = (bf16[256,384]{1,0:T(8,128)(2,1)S(1)}, bf16[256,384]{1,0:T(8,128)(2,1)}, u32[]{:S(2)}) copy-start(bf16[256,384]{1,0:T(8,128)(2,1)} %param.7) | copy-start | bytes 589828
  11.6 25.8 %all-to-all-start = ((bf16[16,32,384]{2,1,0:T(8,128)(2,1)}), bf16[16,32,384]{2,1,0:T(8,128)(2,1)S(1)}, u32[]{:S(2)}, u32[]{:S(2)}) async-start(bf16[16,32,384]{2,1,0:T(8,128)(2,1)} %pad_maximum_fusion), calls=%async_computation | async-start | bytes 786432 | tf_op jit(solution)/shard_map/all_to_all | solution.py:99
  20.2 53.1 %reduce-scatter.2.cloned.1.call-start = ((), (), s32[]{:S(2)}) async-start(), calls=%async_computation.2 | async-start | bytes 2621440 | tf_op jit(solution)/shard_map/reduce_scatter | solution.py:120
  22.9 15.9 %copy-start.1 = (bf16[384,384]{1,0:T(8,128)(2,1)S(1)}, bf16[384,384]{1,0:T(8,128)(2,1)}, u32[]{:S(2)}) copy-start(bf16[384,384]{1,0:T(8,128)(2,1)} %param.8) | copy-start | bytes 884740
  41.0 84.2 %all-gather.3.cloned.1.call-start = ((), (), s32[]{:S(2)}) async-start(), calls=%async_computation.3 | async-start | bytes 1114112 | tf_op jit(solution)/shard_map/all_gather | solution.py:131
Sparse Core Ops, SparseCore 0:
  41.1 32.1 reduce-scatter.1
  76.3 48.8 all-gather.2
where the time goes:
time: 140 us; the launch traced here: 139 us
  waiting for transfers between devices  81.5 us (58%)
  between operations  15 us (11%)
  blocking collectives  14.5 us (10%)
  local copies, waits for them, and re-layouts  9.02 us (6%)
  starting transfers between devices  8.65 us (6%)
  other arithmetic  5.54 us (4%)
  matrix products  5.16 us (4%)
    all_gather x1, waiting for transfers between devices, body(): lax.all_gather(summed[:, query_cols:].astype(jnp.bfloat16), ('row', 'col'...  49.1 us
    reduce_scatter x1, waiting for transfers between devices, body(): lax.psum_scatter(partial_value + jnp.concatenate([adapter_term, jnp.zeros...  32.3 us
    all_gather x1, blocking collectives, body(): gathered = lax.all_gather(hidden_states, 'row', axis=0, tiled=True)  14.5 us
    all_to_all x1, starting transfers between devices, body(): lax.all_to_all(outgoing, 'dp', split_axis=0, concat_axis=0, tiled=True)  8.57 us
  transfers between devices with their start and end apart: 3, of which 2 were waited for; matrix products, arithmetic and copies ran while one was open for 2% of the time, Pallas kernels for 0%

commit v1 on v0

--- a/solution.py
+++ b/solution.py
@@ -7,6 +7,12 @@
 HEAD_DIM = 128
 MOST_LEN = 160
 masked_score = -1e30
+
+
+def joined_along(tiles, dim):
+    shape = list(tiles.shape[1:])
+    shape[dim] *= tiles.shape[0]
+    return jnp.moveaxis(tiles, 0, dim).reshape(shape)
 
 
 def block_layout(lengths_row, block_len):
@@ -69,7 +75,19 @@
     block_index = lax.axis_index("dp")
     col_index = lax.axis_index("col")
     row_index = lax.axis_index("row")
-    gathered = lax.all_gather(hidden_states, "row", axis=0, tiled=True)
+    size = lax.axis_size("row")
+    pairs = [(i, (i + 1) % size) for i in range(size)]
+    back = [(b, a) for a, b in pairs]
+    lower, upper = ([], [])
+    for step in range(size - 1):
+        if step % 2 == 0:
+            lower.append(lax.ppermute(lower[-1] if lower else hidden_states, "row", pairs))
+        else:
+            upper.append(lax.ppermute(upper[-1] if upper else hidden_states, "row", back))
+    pieces = jnp.stack([*lower[::-1], hidden_states, *upper])
+    shift = lax.axis_index("row") - len(lower)
+    pieces = pieces[(jnp.arange(size) - shift) % size]
+    gathered = joined_along(pieces, 0)
     block_len = gathered.shape[0]
     query_cols = w_query.shape[1]
     kv_cols = w_key_value.shape[1]

time: 140 us -> 134 us (0.957)
  blocking collectives: 14.5 us -> 0 us
  waiting for transfers between devices: 81.5 us -> 86.4 us
  starting transfers between devices: 8.65 us -> 12.4 us
    all_gather x1 -> x0, blocking collectives: 14.5 us -> none  [body(): gathered = lax.all_gather(hidden_states, 'row', axis=0, tiled=True)]
    ppermute x0 -> x3, waiting for transfers between devices: none -> 8.06 us  [the longest x2 8.05 us: body(): lax.ppermute(lower[-1] if lower else hidden_states, 'row', pairs)]
    reduce_scatter x1, waiting for transfers between devices: 32.3 us -> 28.5 us  [body(): lax.psum_scatter(partial_value + jnp.concatenate([adapter_term, jnp.zeros...]
    ppermute x0 -> x3, starting transfers between devices: none -> 3.76 us  [the longest x2 2.1 us: body(): lax.ppermute(lower[-1] if lower else hidden_states, 'row', pairs)]
    reshape x1 -> x0, local copies, waits for them, and re-layouts: 1.85 us -> none  [body(): kv_pieces.reshape(lax.axis_size('row'), lax.axis_size('col'), own_rows, k...]
    all_to_all x1, waiting for transfers between devices: 0.01 us -> 1.51 us  [body(): lax.all_to_all(outgoing, 'dp', split_axis=0, concat_axis=0, tiled=True)]
  transfers between devices with their start and end apart: 3 -> 6, of which waited for: 2 -> 4; matrix products, arithmetic and copies ran while one was open for 2% -> 6% of each run, Pallas kernels for 0% -> 0%
where the time goes in v1:
time: 134 us; the launch traced here: 133 us
  waiting for transfers between devices  86.4 us (64%)
  between operations  15 us (11%)
  starting transfers between devices  12.4 us (9%)
  local copies, waits for them, and re-layouts  8.73 us (7%)
  other arithmetic  5.62 us (4%)
  matrix products  5.2 us (4%)
    all_gather x1, waiting for transfers between devices, body(): lax.all_gather(summed[:, query_cols:].astype(jnp.bfloat16), ('row', 'col'...  48.3 us
    reduce_scatter x1, waiting for transfers between devices, body(): lax.psum_scatter(partial_value + jnp.concatenate([adapter_term, jnp.zeros...  28.5 us
    all_to_all x1, starting transfers between devices, body(): lax.all_to_all(outgoing, 'dp', split_axis=0, concat_axis=0, tiled=True)  8.57 us
    ppermute x2, waiting for transfers between devices, body(): lax.ppermute(lower[-1] if lower else hidden_states, 'row', pairs)  8.05 us
  transfers between devices with their start and end apart: 6, of which 4 were waited for; matrix products, arithmetic and copies ran while one was open for 6% of the time, Pallas kernels for 0%

profile of v1, /device:TPU:2, one launch (start us, length us, event | category | flops | bytes accessed | tf_op | source)
XLA Modules:
  0.0 133.4 jit_solution(2715863369448770258)
XLA Ops:
  7.2 0.0 copy-start
  7.2 0.0 copy-start.2
  7.2 1.7 %collective-permute-start = (bf16[256,384]{1,0:T(8,128)(2,1)}, bf16[256,384]{1,0:T(8,128)(2,1)S(1)}, u32[]{:S(2)}, u32[]{:S(2)}) collective-permute-start(bf16[256,384]{1,0:T(8,128)(2,1)} %param.7), channel_id=1, source_target_pairs={{0,64},{64,128},{128,192},{192,0},{1,65},{65,129},{129,193},{193,1... | collective-permute-start | bytes 589832 | tf_op jit(solution)/shard_map/ppermute | solution.py:84
  8.9 1.7 %collective-permute-start.2 = (bf16[256,384]{1,0:T(8,128)(2,1)}, bf16[256,384]{1,0:T(8,128)(2,1)S(1)}, u32[]{:S(2)}, u32[]{:S(2)}) collective-permute-start(bf16[256,384]{1,0:T(8,128)(2,1)} %param.7), channel_id=1, source_target_pairs={{64,0},{128,64},{192,128},{0,192},{65,1},{129,65},{193,129},{1,193... | collective-permute-start | bytes 589832 | tf_op jit(solution)/shard_map/ppermute | solution.py:86
  10.5 0.7 fusion.24
  11.3 0.6 gather_fusion.2
  11.9 1.7 %gather_fusion.1 = bf16[16,384,16]{1,2,0:T(8,128)(2,1)S(1)} fusion(bf16[64,384,16]{1,2,0:T(8,128)(2,1)} %param.10, s32[1024]{0:T(1024)S(1)} %pad_clamp_fusion), kind=kCustom, calls=%fused_computation.1 | custom fusion | bytes 393280 | tf_op jit(solution)/shard_map/jit(_take)/gather | solution.py:114
  13.6 0.1 broadcast_select_fusion
  13.7 0.1 select_bitcast_fusion
  13.8 0.8 pad_maximum_fusion.1
  14.6 8.6 %all-to-all-start = ((bf16[16,32,384]{2,1,0:T(8,128)(2,1)}), bf16[16,32,384]{2,1,0:T(8,128)(2,1)S(1)}, u32[]{:S(2)}, u32[]{:S(2)}) async-start(bf16[16,32,384]{2,1,0:T(8,128)(2,1)} %pad_maximum_fusion.1), calls=%async_computation | async-start | bytes 786432 | tf_op jit(solution)/shard_map/all_to_all | solution.py:117
  23.2 0.0 reduce-scatter.2.cloned.1.call-start
  23.3 0.7 fusion.35
  24.7 0.1 subtract_reduce_fusion
  24.8 0.1 convert_reduce_fusion
  24.9 0.9 constant_dynamic-slice_fusion.2
  25.8 0.1 select_reduce_fusion
  25.9 0.0 collective-permute-done
  25.9 0.4 collective-permute-start.1
  26.4 0.0 collective-permute-done.2
  26.4 8.1 %collective-permute-done.1 = bf16[256,384]{1,0:T(8,128)(2,1)S(1)} collective-permute-done((bf16[256,384]{1,0:T(8,128)(2,1)S(1)}, bf16[256,384]{1,0:T(8,128)(2,1)S(1)}, u32[]{:S(2)}, u32[]{:S(2)}) %collective-permute-start.1) | collective-permute-done | bytes 196640 | tf_op jit(solution)/shard_map/ppermute | solution.py:84
  34.4 0.0 copy-done.2
  34.4 0.1 pad_maximum_fusion
  34.6 0.7 gather_fusion
  35.3 0.0 copy-start.1
  35.3 1.5 %all-to-all-done = bf16[16,32,384]{2,1,0:T(8,128)(2,1)S(1)} async-done(((bf16[16,32,384]{2,1,0:T(8,128)(2,1)}), bf16[16,32,384]{2,1,0:T(8,128)(2,1)S(1)}, u32[]{:S(2)}, u32[]{:S(2)}) %all-to-all-start) | async-done | bytes 393248 | tf_op jit(solution)/shard_map/all_to_all | solution.py:117
  36.8 0.5 convolution_select_fusion
  37.3 1.0 fusion.37
  38.3 0.0 copy-done.1
  38.3 2.1 %pad_add_fusion = f32[1024,512]{1,0:T(8,128)} fusion(f32[1024,384]{1,0:T(8,128)S(1)} %fusion.37, bf16[1024,384]{1,0:T(8,128)(2,1)S(1)} %bitcast.65, bf16[384,128]{1,0:T(8,128)(2,1)S(1)} %constant_dynamic-slice_fusion.2, bf16[384,384]{1,0:T(8,128)(2,1)S(1)} %copy-done.1), kind=kOutput, calls=%fused_computation.8 | convolution fusion | flops 403963904 | bytes 4849664 | tf_op jit(solution)/shard_map/dot_general | solution.py:137
  40.4 0.0 reduce-scatter.2.cloned.1.call-update
  40.4 0.0 all-gather.3.cloned.1.call-start
  40.5 28.5 %reduce-scatter.2.cloned.1.call-done = f32[256,512]{1,0:T(8,128)} async-done(((f32[1024,512]{1,0:T(8,128)}), f32[256,512]{1,0:T(8,128)}) %reduce-scatter.2.cloned.1.call-update) | async-done | bytes 524304 | tf_op jit(solution)/shard_map/reduce_scatter | solution.py:138
  68.9 1.1 convert.4
  70.0 0.6 slice.26
  70.6 0.0 all-gather.3.cloned.1.call-update
  70.7 0.1 dynamic_slice.23
  70.8 0.8 fusion.9
  71.6 0.1 copy.27
  71.8 48.3 %all-gather.3.cloned.1.call-done = bf16[4096,128]{1,0:T(8,128)(2,1)} async-done(((bf16[256,128]{1,0:T(8,128)(2,1)}), bf16[4096,128]{1,0:T(8,128)(2,1)}) %all-gather.3.cloned.1.call-update) | async-done | bytes 1048592 | tf_op jit(solution)/shard_map/all_gather | solution.py:149
  120.1 1.0 dynamic-slice_bitcast_fusion
  121.1 0.1 copy.32
  121.3 0.8 copy.34
  122.1 1.1 constant_dynamic-slice_fusion.1
  123.2 0.7 fusion
  123.9 0.8 fusion.1
  124.7 1.0 fusion.13
  125.7 0.8 copy.33
  (19 shorter events, 0.2 us)
Async XLA Ops:
  7.2 4.1 %copy-start = (bf16[64,16,384]{2,1,0:T(8,128)(2,1)S(1)}, bf16[64,16,384]{2,1,0:T(8,128)(2,1)}, u32[]{:S(2)}) copy-start(bf16[64,16,384]{2,1,0:T(8,128)(2,1)} %param.11) | copy-start | bytes 2359300
  7.2 27.2 %copy-start.2 = (bf16[256,384]{1,0:T(8,128)(2,1)S(1)}, bf16[256,384]{1,0:T(8,128)(2,1)}, u32[]{:S(2)}) copy-start(bf16[256,384]{1,0:T(8,128)(2,1)} %param.7) | copy-start | bytes 589828
  7.2 16.1 %copy-start.3 = (s32[16,8]{0,1:T(8,128)S(1)}, s32[16,8]{0,1:T(8,128)}, u32[]{:S(2)}) copy-start(s32[16,8]{0,1:T(8,128)} %param.13) | copy-start | bytes 1540
  7.2 16.1 %copy-start.4 = (s32[16,8]{0,1:T(8,128)S(1)}, s32[16,8]{0,1:T(8,128)}, u32[]{:S(2)}) copy-start(s32[16,8]{0,1:T(8,128)} %param.12) | copy-start | bytes 1540
  7.2 18.7 %collective-permute-start = (bf16[256,384]{1,0:T(8,128)(2,1)}, bf16[256,384]{1,0:T(8,128)(2,1)S(1)}, u32[]{:S(2)}, u32[]{:S(2)}) collective-permute-start(bf16[256,384]{1,0:T(8,128)(2,1)} %param.7), channel_id=1, source_target_pairs={{0,64},{64,128},{128,192},{192,0},{1,65},{65,129},{129,193},{193,1... | collective-permute-start | bytes 589832 | tf_op jit(solution)/shard_map/ppermute | solution.py:84
  8.9 17.5 %collective-permute-start.2 = (bf16[256,384]{1,0:T(8,128)(2,1)}, bf16[256,384]{1,0:T(8,128)(2,1)S(1)}, u32[]{:S(2)}, u32[]{:S(2)}) collective-permute-start(bf16[256,384]{1,0:T(8,128)(2,1)} %param.7), channel_id=1, source_target_pairs={{64,0},{128,64},{192,128},{0,192},{65,1},{129,65},{193,129},{1,193... | collective-permute-start | bytes 589832 | tf_op jit(solution)/shard_map/ppermute | solution.py:86
  14.6 22.2 %all-to-all-start = ((bf16[16,32,384]{2,1,0:T(8,128)(2,1)}), bf16[16,32,384]{2,1,0:T(8,128)(2,1)S(1)}, u32[]{:S(2)}, u32[]{:S(2)}) async-start(bf16[16,32,384]{2,1,0:T(8,128)(2,1)} %pad_maximum_fusion.1), calls=%async_computation | async-start | bytes 786432 | tf_op jit(solution)/shard_map/all_to_all | solution.py:117
  23.2 45.8 %reduce-scatter.2.cloned.1.call-start = ((), (), s32[]{:S(2)}) async-start(), calls=%async_computation.2 | async-start | bytes 2621440 | tf_op jit(solution)/shard_map/reduce_scatter | solution.py:138
  25.9 8.5 %collective-permute-start.1 = (bf16[256,384]{1,0:T(8,128)(2,1)S(1)}, bf16[256,384]{1,0:T(8,128)(2,1)S(1)}, u32[]{:S(2)}, u32[]{:S(2)}) collective-permute-start(bf16[256,384]{1,0:T(8,128)(2,1)S(1)} %collective-permute-done), channel_id=1, source_target_pairs={{0,64},{64,128},{128,192},{192,0},{1,65},{65,129},{129,193},{193,1... | collective-permute-start | bytes 589832 | tf_op jit(solution)/shard_map/ppermute | solution.py:84
  35.3 3.0 %copy-start.1 = (bf16[384,384]{1,0:T(8,128)(2,1)S(1)}, bf16[384,384]{1,0:T(8,128)(2,1)}, u32[]{:S(2)}) copy-start(bf16[384,384]{1,0:T(8,128)(2,1)} %param.8) | copy-start | bytes 884740
  40.4 79.7 %all-gather.3.cloned.1.call-start = ((), (), s32[]{:S(2)}) async-start(), calls=%async_computation.3 | async-start | bytes 1114112 | tf_op jit(solution)/shard_map/all_gather | solution.py:149
Sparse Core Ops, SparseCore 0:
  40.5 28.3 reduce-scatter.1
  71.9 48.1 all-gather.2
